TPU v7x, 512 devices: a whole 4x8x8 slice. The times are simulated.
512 devices in a mesh: ctx: 64 (over y, x, core), head: 8 (over z).
Axes of the slice: x: 4, y: 8, z: 8, core: 2. Of those that a mesh axis runs over, the one named last changes fastest.
Arguments:
- tokens: bfloat16 [65536, 2048], P('ctx', 'head'), may hold values from -6 to 6
- w_qkv: bfloat16 [3, 2048, 2048], P(None, 'ctx', 'head'), may hold values from -0.125 to 0.125
- out_gain: float32 [2048], P('head'), may hold values from 0.25 to 1.75
- seg_ids: int32 [65536], P('ctx'), may hold values from 0 to 15, never falling along the last dimension, each value on 1 to 16384 neighbouring positions
Outputs:
- attended: bfloat16 [65536, 2048], P('ctx', 'head')
Inputs may be any that keep to these rules, and one draw needn't show every extreme that they name: `seg_ids`: segment numbers never fall along the stream; each segment covers 1 to 16384 consecutive tokens, and one covers exactly 16384.
All inputs are finite; a program needn't handle non-finite values.
Results may differ from a plain program's by a relative error of at most 0.012.
Values may be sent and summed in bfloat16 or wider, within the bound.
No kernel may reach another device: no remote copies, remote signals or barrier semaphores. Data moves between devices by JAX's collectives and lax.ppermute only.
A program may use at most 64 MiB of HBM per device.

v0:
```python
import jax
import jax.numpy as jnp
from jax import lax
from jax.sharding import PartitionSpec as P

HEAD_DIM = 128


def passed_along(value, axis, steps):
    count = lax.axis_size(axis)
    leading, last = (max(0, -steps), min(count, count - steps))
    return lax.ppermute(value, axis, [(source, source + steps) for source in range(leading, last)])


def feature_map(values):
    return (jax.nn.elu(values.astype(jnp.float32)) + 1.0).astype(jnp.bfloat16)


def combine(earlier, later):
    first_state, first_tail = earlier
    later_state, later_tail = later
    linked = (first_tail == later_tail) | (later_tail < 0.0)
    return (
        later_state + jnp.where(linked, first_state, 0.0),
        jnp.where(later_tail < 0.0, first_tail, later_tail),
    )


def prepare(projected, segment):
    row_count = segment.shape[0]
    head_count = projected.shape[2] // HEAD_DIM
    queries = feature_map(projected[0]).reshape(row_count, head_count, HEAD_DIM)
    key_map = feature_map(projected[1]).reshape(row_count, head_count, HEAD_DIM)
    values = projected[2].reshape(row_count, head_count, HEAD_DIM)
    seg_float = segment.astype(jnp.float32)
    tail_id = seg_float[-1]
    key_tail = jnp.where((seg_float == tail_id)[:, None, None], key_map, jnp.zeros_like(key_map))
    kv_state = jnp.einsum("thd,the->hde", key_tail, values, preferred_element_type=jnp.float32)
    return (queries, key_map, values, seg_float, kv_state, tail_id)


def complete(queries, key_map, values, seg_float, state_in, tail_in, out_gain):
    row_count, head_count = (queries.shape[0], queries.shape[1])
    state_low = state_in.astype(jnp.bfloat16)
    prefix = jnp.einsum("thd,hde->the", queries, state_low, preferred_element_type=jnp.float32)
    prefix = jnp.where((seg_float == tail_in)[:, None, None], prefix, 0.0)
    block_rows = min(512, row_count)
    positions = jnp.arange(row_count, dtype=jnp.int32)

    def one_block(blk_no):
        first_row = blk_no * block_rows
        query_blk = lax.dynamic_slice_in_dim(queries, first_row, block_rows, 0)
        query_pos = first_row + jnp.arange(block_rows, dtype=jnp.int32)
        query_seg = lax.dynamic_slice_in_dim(seg_float, first_row, block_rows, 0)
        scores = jnp.einsum("bhd,shd->hbs", query_blk, key_map, preferred_element_type=jnp.float32)
        visible = (positions[None, :] <= query_pos[:, None]) & (
            seg_float[None, :] == query_seg[:, None]
        )
        weights = jnp.where(visible[None], scores, 0.0).astype(jnp.bfloat16)
        return jnp.einsum("hbs,she->bhe", weights, values, preferred_element_type=jnp.float32)

    local_part = lax.map(one_block, jnp.arange(row_count // block_rows, dtype=jnp.int32))
    numerator = local_part.reshape(row_count, head_count, HEAD_DIM) + prefix
    inv_norm = lax.rsqrt(jnp.mean(numerator * numerator, axis=-1, keepdims=True) + 1e-05)
    result = numerator * inv_norm * out_gain.reshape(head_count, HEAD_DIM)
    return result.astype(jnp.bfloat16).reshape(row_count, head_count * HEAD_DIM)


def per_device(tokens, w_qkv, out_gain, seg_ids):
    whole = lax.all_gather(tokens, "head", axis=1, tiled=True)
    projected = jnp.einsum(
        "tr,grc->gtc",
        whole,
        lax.all_gather(w_qkv, "ctx", axis=1, tiled=True),
        preferred_element_type=jnp.float32,
    ).astype(jnp.bfloat16)
    queries, key_map, values, seg_float, kv_state, tail_id = prepare(projected, seg_ids)
    empty_state = jnp.zeros_like(kv_state)
    own_pair = (kv_state, tail_id)

    def hand_round(turn_no, carried):
        running, _ = carried
        incoming = (
            passed_along(running[0].astype(jnp.bfloat16), "ctx", 1).astype(jnp.float32),
            passed_along(running[1].astype(jnp.bfloat16), "ctx", 1).astype(jnp.float32),
        )
        return (combine(incoming, own_pair), incoming)

    start_pair = (empty_state, jnp.array(-1.0, jnp.float32))
    _, arrived = lax.fori_loop(0, lax.axis_size("ctx") - 1, hand_round, (own_pair, start_pair))
    state_in, tail_in = arrived
    return complete(queries, key_map, values, seg_float, state_in, tail_in, out_gain)


def solution(mesh):
    placed = (P("ctx", "head"), P(None, "ctx", "head"), P("head"), P("ctx"))
    return jax.shard_map(
        per_device, mesh=mesh, in_specs=placed, out_specs=P("ctx", "head"), check_vma=False
    )
```

profile of v0, /device:TPU:32, one launch (start us, length us, event | category | flops | bytes accessed | tf_op | source)
XLA Modules:
  0.0 1084.5 jit_solution(1804793181118891656)
XLA Ops:
  12.1 84.4 %all-gather.3.cloned.1.call-done = bf16[3,2048,256]{2,1,0:T(8,128)(2,1)} async-done(((bf16[3,32,256]{2,1,0:T(8,128)(2,1)}), bf16[3,2048,256]{2,1,0:T(8,128)(2,1)}) %all-gather.3.cloned.1.call-update) | async-done | bytes 3145744 | tf_op jit(solution)/shard_map/all_gather | solution.py:74
  96.5 67.6 %all-gather.5.cloned.1.call-done = bf16[1024,2048]{1,0:T(8,128)(2,1)} async-done(((bf16[1024,256]{1,0:T(8,128)(2,1)}), bf16[1024,2048]{1,0:T(8,128)(2,1)}) %all-gather.5.cloned.1.call-update) | async-done | bytes 4194320 | tf_op jit(solution)/shard_map/all_gather | solution.py:70
  164.0 6.6 fusion.15
  176.5 877.2 %while.28 = (s32[]{:T(128)}, bf16[2,128,128]{2,1,0:T(8,128)(2,1)S(1)}, bf16[]{:T(256)}, bf16[2,128,128]{2,1,0:T(8,128)(2,1)}, f32[]{:T(128)}, /*index=5*/f32[]{:...) while((s32[]{:T(128)}, bf16[2,128,128]{2,1,0:T(8,128)(2,1)S(1)}, bf16[]{:T(256)}, ...), condition=%wide.region_3.4_spmd, body=%wide.region_2.3_spmd.sunk | while | flops 163846 | bytes 590031 | solution.py:90
  195.3 5.4 collective-permute-done
  209.2 5.4 collective-permute-done
  223.1 5.4 collective-permute-done
  264.9 5.4 collective-permute-done
  278.8 5.4 collective-permute-done
  292.7 5.4 collective-permute-done
  306.6 5.4 collective-permute-done
  320.6 5.4 collective-permute-done
  334.5 5.4 collective-permute-done
  348.4 5.4 collective-permute-done
  362.3 5.4 collective-permute-done
  404.1 5.4 collective-permute-done
  418.0 5.4 collective-permute-done
  432.0 5.4 collective-permute-done
  445.9 5.4 collective-permute-done
  459.8 5.4 collective-permute-done
  473.7 5.4 collective-permute-done
  487.6 5.4 collective-permute-done
  529.4 5.4 collective-permute-done
  543.3 5.4 collective-permute-done
  557.3 5.4 collective-permute-done
  571.2 5.4 collective-permute-done
  585.1 5.4 collective-permute-done
  599.0 5.4 collective-permute-done
  613.0 5.4 collective-permute-done
  626.9 5.4 collective-permute-done
  668.6 5.4 collective-permute-done
  1056.0 19.2 %while.29 = (s32[]{:T(128)}, f32[2,512,2,128]{1,0,3,2:T(2,128)S(1)}, s32[2]{0:T(128)S(1)}, f32[1024]{0:T(1024)S(1)}, bf16[1024,2,128]{2,1,0:T(2,128)(2,1)S(1)}, ...) while((s32[]{:T(128)}, ...), condition=%wide.region_1.2_spmd.clone, body=%wide.region_0.1_spmd.clone.sunk | while | flops 540541440 | bytes 5519551 | solution.py:62
  (335 shorter events, 568.7 us)
Async XLA Ops:
  6.5 89.9 %all-gather.3.cloned.1.call-start = ((), (), s32[]{:S(2)}) async-start(), calls=%async_computation | async-start | bytes 3194880 | tf_op jit(solution)/shard_map/all_gather | solution.py:74
  7.3 156.8 %all-gather.5.cloned.1.call-start = ((), (), s32[]{:S(2)}) async-start(), calls=%async_computation.1 | async-start | bytes 4718592 | tf_op jit(solution)/shard_map/all_gather | solution.py:70
  176.5 13.3 %collective-permute-start.1 = (bf16[2,128,128]{2,1,0:T(8,128)(2,1)S(1)}, bf16[2,128,128]{2,1,0:T(8,128)(2,1)S(1)}, u32[]{:S(2)}, u32[]{:S(2)}) collective-permute-start(bf16[2,128,128]{2,1,0:T(8,128)(2,1)S(1)} %get-tuple-element.318), channel_id=1, source_target_pairs={{0,8},{8,16},{16,24},{24,32},{32,40},{40,48},{48,56},{56,64},{64,7... | collective-permute-start | bytes 196616 | tf_op jit(solution)/shard_map/while/body/eval_jaxpr/ppermute | solution.py:12
  190.5 13.3 %collective-permute-start.1 = (bf16[2,128,128]{2,1,0:T(8,128)(2,1)S(1)}, bf16[2,128,128]{2,1,0:T(8,128)(2,1)S(1)}, u32[]{:S(2)}, u32[]{:S(2)}) collective-permute-start(bf16[2,128,128]{2,1,0:T(8,128)(2,1)S(1)} %get-tuple-element.318), channel_id=1, source_target_pairs={{0,8},{8,16},{16,24},{24,32},{32,40},{40,48},{48,56},{56,64},{64,7... | collective-permute-start | bytes 196616 | tf_op jit(solution)/shard_map/while/body/eval_jaxpr/ppermute | solution.py:12
  204.4 13.3 %collective-permute-start.1 = (bf16[2,128,128]{2,1,0:T(8,128)(2,1)S(1)}, bf16[2,128,128]{2,1,0:T(8,128)(2,1)S(1)}, u32[]{:S(2)}, u32[]{:S(2)}) collective-permute-start(bf16[2,128,128]{2,1,0:T(8,128)(2,1)S(1)} %get-tuple-element.318), channel_id=1, source_target_pairs={{0,8},{8,16},{16,24},{24,32},{32,40},{40,48},{48,56},{56,64},{64,7... | collective-permute-start | bytes 196616 | tf_op jit(solution)/shard_map/while/body/eval_jaxpr/ppermute | solution.py:12
  218.3 13.3 %collective-permute-start.1 = (bf16[2,128,128]{2,1,0:T(8,128)(2,1)S(1)}, bf16[2,128,128]{2,1,0:T(8,128)(2,1)S(1)}, u32[]{:S(2)}, u32[]{:S(2)}) collective-permute-start(bf16[2,128,128]{2,1,0:T(8,128)(2,1)S(1)} %get-tuple-element.318), channel_id=1, source_target_pairs={{0,8},{8,16},{16,24},{24,32},{32,40},{40,48},{48,56},{56,64},{64,7... | collective-permute-start | bytes 196616 | tf_op jit(solution)/shard_map/while/body/eval_jaxpr/ppermute | solution.py:12
  287.9 13.3 %collective-permute-start.1 = (bf16[2,128,128]{2,1,0:T(8,128)(2,1)S(1)}, bf16[2,128,128]{2,1,0:T(8,128)(2,1)S(1)}, u32[]{:S(2)}, u32[]{:S(2)}) collective-permute-start(bf16[2,128,128]{2,1,0:T(8,128)(2,1)S(1)} %get-tuple-element.318), channel_id=1, source_target_pairs={{0,8},{8,16},{16,24},{24,32},{32,40},{40,48},{48,56},{56,64},{64,7... | collective-permute-start | bytes 196616 | tf_op jit(solution)/shard_map/while/body/eval_jaxpr/ppermute | solution.py:12
  301.9 13.3 %collective-permute-start.1 = (bf16[2,128,128]{2,1,0:T(8,128)(2,1)S(1)}, bf16[2,128,128]{2,1,0:T(8,128)(2,1)S(1)}, u32[]{:S(2)}, u32[]{:S(2)}) collective-permute-start(bf16[2,128,128]{2,1,0:T(8,128)(2,1)S(1)} %get-tuple-element.318), channel_id=1, source_target_pairs={{0,8},{8,16},{16,24},{24,32},{32,40},{40,48},{48,56},{56,64},{64,7... | collective-permute-start | bytes 196616 | tf_op jit(solution)/shard_map/while/body/eval_jaxpr/ppermute | solution.py:12
  315.8 13.3 %collective-permute-start.1 = (bf16[2,128,128]{2,1,0:T(8,128)(2,1)S(1)}, bf16[2,128,128]{2,1,0:T(8,128)(2,1)S(1)}, u32[]{:S(2)}, u32[]{:S(2)}) collective-permute-start(bf16[2,128,128]{2,1,0:T(8,128)(2,1)S(1)} %get-tuple-element.318), channel_id=1, source_target_pairs={{0,8},{8,16},{16,24},{24,32},{32,40},{40,48},{48,56},{56,64},{64,7... | collective-permute-start | bytes 196616 | tf_op jit(solution)/shard_map/while/body/eval_jaxpr/ppermute | solution.py:12
  329.7 13.3 %collective-permute-start.1 = (bf16[2,128,128]{2,1,0:T(8,128)(2,1)S(1)}, bf16[2,128,128]{2,1,0:T(8,128)(2,1)S(1)}, u32[]{:S(2)}, u32[]{:S(2)}) collective-permute-start(bf16[2,128,128]{2,1,0:T(8,128)(2,1)S(1)} %get-tuple-element.318), channel_id=1, source_target_pairs={{0,8},{8,16},{16,24},{24,32},{32,40},{40,48},{48,56},{56,64},{64,7... | collective-permute-start | bytes 196616 | tf_op jit(solution)/shard_map/while/body/eval_jaxpr/ppermute | solution.py:12
  343.6 13.3 %collective-permute-start.1 = (bf16[2,128,128]{2,1,0:T(8,128)(2,1)S(1)}, bf16[2,128,128]{2,1,0:T(8,128)(2,1)S(1)}, u32[]{:S(2)}, u32[]{:S(2)}) collective-permute-start(bf16[2,128,128]{2,1,0:T(8,128)(2,1)S(1)} %get-tuple-element.318), channel_id=1, source_target_pairs={{0,8},{8,16},{16,24},{24,32},{32,40},{40,48},{48,56},{56,64},{64,7... | collective-permute-start | bytes 196616 | tf_op jit(solution)/shard_map/while/body/eval_jaxpr/ppermute | solution.py:12
  413.3 13.3 %collective-permute-start.1 = (bf16[2,128,128]{2,1,0:T(8,128)(2,1)S(1)}, bf16[2,128,128]{2,1,0:T(8,128)(2,1)S(1)}, u32[]{:S(2)}, u32[]{:S(2)}) collective-permute-start(bf16[2,128,128]{2,1,0:T(8,128)(2,1)S(1)} %get-tuple-element.318), channel_id=1, source_target_pairs={{0,8},{8,16},{16,24},{24,32},{32,40},{40,48},{48,56},{56,64},{64,7... | collective-permute-start | bytes 196616 | tf_op jit(solution)/shard_map/while/body/eval_jaxpr/ppermute | solution.py:12
  427.2 13.3 %collective-permute-start.1 = (bf16[2,128,128]{2,1,0:T(8,128)(2,1)S(1)}, bf16[2,128,128]{2,1,0:T(8,128)(2,1)S(1)}, u32[]{:S(2)}, u32[]{:S(2)}) collective-permute-start(bf16[2,128,128]{2,1,0:T(8,128)(2,1)S(1)} %get-tuple-element.318), channel_id=1, source_target_pairs={{0,8},{8,16},{16,24},{24,32},{32,40},{40,48},{48,56},{56,64},{64,7... | collective-permute-start | bytes 196616 | tf_op jit(solution)/shard_map/while/body/eval_jaxpr/ppermute | solution.py:12
  441.1 13.3 %collective-permute-start.1 = (bf16[2,128,128]{2,1,0:T(8,128)(2,1)S(1)}, bf16[2,128,128]{2,1,0:T(8,128)(2,1)S(1)}, u32[]{:S(2)}, u32[]{:S(2)}) collective-permute-start(bf16[2,128,128]{2,1,0:T(8,128)(2,1)S(1)} %get-tuple-element.318), channel_id=1, source_target_pairs={{0,8},{8,16},{16,24},{24,32},{32,40},{40,48},{48,56},{56,64},{64,7... | collective-permute-start | bytes 196616 | tf_op jit(solution)/shard_map/while/body/eval_jaxpr/ppermute | solution.py:12
  455.0 13.3 %collective-permute-start.1 = (bf16[2,128,128]{2,1,0:T(8,128)(2,1)S(1)}, bf16[2,128,128]{2,1,0:T(8,128)(2,1)S(1)}, u32[]{:S(2)}, u32[]{:S(2)}) collective-permute-start(bf16[2,128,128]{2,1,0:T(8,128)(2,1)S(1)} %get-tuple-element.318), channel_id=1, source_target_pairs={{0,8},{8,16},{16,24},{24,32},{32,40},{40,48},{48,56},{56,64},{64,7... | collective-permute-start | bytes 196616 | tf_op jit(solution)/shard_map/while/body/eval_jaxpr/ppermute | solution.py:12
  468.9 13.3 %collective-permute-start.1 = (bf16[2,128,128]{2,1,0:T(8,128)(2,1)S(1)}, bf16[2,128,128]{2,1,0:T(8,128)(2,1)S(1)}, u32[]{:S(2)}, u32[]{:S(2)}) collective-permute-start(bf16[2,128,128]{2,1,0:T(8,128)(2,1)S(1)} %get-tuple-element.318), channel_id=1, source_target_pairs={{0,8},{8,16},{16,24},{24,32},{32,40},{40,48},{48,56},{56,64},{64,7... | collective-permute-start | bytes 196616 | tf_op jit(solution)/shard_map/while/body/eval_jaxpr/ppermute | solution.py:12
  482.9 13.3 %collective-permute-start.1 = (bf16[2,128,128]{2,1,0:T(8,128)(2,1)S(1)}, bf16[2,128,128]{2,1,0:T(8,128)(2,1)S(1)}, u32[]{:S(2)}, u32[]{:S(2)}) collective-permute-start(bf16[2,128,128]{2,1,0:T(8,128)(2,1)S(1)} %get-tuple-element.318), channel_id=1, source_target_pairs={{0,8},{8,16},{16,24},{24,32},{32,40},{40,48},{48,56},{56,64},{64,7... | collective-permute-start | bytes 196616 | tf_op jit(solution)/shard_map/while/body/eval_jaxpr/ppermute | solution.py:12
  552.5 13.3 %collective-permute-start.1 = (bf16[2,128,128]{2,1,0:T(8,128)(2,1)S(1)}, bf16[2,128,128]{2,1,0:T(8,128)(2,1)S(1)}, u32[]{:S(2)}, u32[]{:S(2)}) collective-permute-start(bf16[2,128,128]{2,1,0:T(8,128)(2,1)S(1)} %get-tuple-element.318), channel_id=1, source_target_pairs={{0,8},{8,16},{16,24},{24,32},{32,40},{40,48},{48,56},{56,64},{64,7... | collective-permute-start | bytes 196616 | tf_op jit(solution)/shard_map/while/body/eval_jaxpr/ppermute | solution.py:12
  566.4 13.3 %collective-permute-start.1 = (bf16[2,128,128]{2,1,0:T(8,128)(2,1)S(1)}, bf16[2,128,128]{2,1,0:T(8,128)(2,1)S(1)}, u32[]{:S(2)}, u32[]{:S(2)}) collective-permute-start(bf16[2,128,128]{2,1,0:T(8,128)(2,1)S(1)} %get-tuple-element.318), channel_id=1, source_target_pairs={{0,8},{8,16},{16,24},{24,32},{32,40},{40,48},{48,56},{56,64},{64,7... | collective-permute-start | bytes 196616 | tf_op jit(solution)/shard_map/while/body/eval_jaxpr/ppermute | solution.py:12
  580.3 13.3 %collective-permute-start.1 = (bf16[2,128,128]{2,1,0:T(8,128)(2,1)S(1)}, bf16[2,128,128]{2,1,0:T(8,128)(2,1)S(1)}, u32[]{:S(2)}, u32[]{:S(2)}) collective-permute-start(bf16[2,128,128]{2,1,0:T(8,128)(2,1)S(1)} %get-tuple-element.318), channel_id=1, source_target_pairs={{0,8},{8,16},{16,24},{24,32},{32,40},{40,48},{48,56},{56,64},{64,7... | collective-permute-start | bytes 196616 | tf_op jit(solution)/shard_map/while/body/eval_jaxpr/ppermute | solution.py:12
  594.3 13.3 %collective-permute-start.1 = (bf16[2,128,128]{2,1,0:T(8,128)(2,1)S(1)}, bf16[2,128,128]{2,1,0:T(8,128)(2,1)S(1)}, u32[]{:S(2)}, u32[]{:S(2)}) collective-permute-start(bf16[2,128,128]{2,1,0:T(8,128)(2,1)S(1)} %get-tuple-element.318), channel_id=1, source_target_pairs={{0,8},{8,16},{16,24},{24,32},{32,40},{40,48},{48,56},{56,64},{64,7... | collective-permute-start | bytes 196616 | tf_op jit(solution)/shard_map/while/body/eval_jaxpr/ppermute | solution.py:12
  608.2 13.3 %collective-permute-start.1 = (bf16[2,128,128]{2,1,0:T(8,128)(2,1)S(1)}, bf16[2,128,128]{2,1,0:T(8,128)(2,1)S(1)}, u32[]{:S(2)}, u32[]{:S(2)}) collective-permute-start(bf16[2,128,128]{2,1,0:T(8,128)(2,1)S(1)} %get-tuple-element.318), channel_id=1, source_target_pairs={{0,8},{8,16},{16,24},{24,32},{32,40},{40,48},{48,56},{56,64},{64,7... | collective-permute-start | bytes 196616 | tf_op jit(solution)/shard_map/while/body/eval_jaxpr/ppermute | solution.py:12
  677.8 13.3 %collective-permute-start.1 = (bf16[2,128,128]{2,1,0:T(8,128)(2,1)S(1)}, bf16[2,128,128]{2,1,0:T(8,128)(2,1)S(1)}, u32[]{:S(2)}, u32[]{:S(2)}) collective-permute-start(bf16[2,128,128]{2,1,0:T(8,128)(2,1)S(1)} %get-tuple-element.318), channel_id=1, source_target_pairs={{0,8},{8,16},{16,24},{24,32},{32,40},{40,48},{48,56},{56,64},{64,7... | collective-permute-start | bytes 196616 | tf_op jit(solution)/shard_map/while/body/eval_jaxpr/ppermute | solution.py:12
  691.7 13.3 %collective-permute-start.1 = (bf16[2,128,128]{2,1,0:T(8,128)(2,1)S(1)}, bf16[2,128,128]{2,1,0:T(8,128)(2,1)S(1)}, u32[]{:S(2)}, u32[]{:S(2)}) collective-permute-start(bf16[2,128,128]{2,1,0:T(8,128)(2,1)S(1)} %get-tuple-element.318), channel_id=1, source_target_pairs={{0,8},{8,16},{16,24},{24,32},{32,40},{40,48},{48,56},{56,64},{64,7... | collective-permute-start | bytes 196616 | tf_op jit(solution)/shard_map/while/body/eval_jaxpr/ppermute | solution.py:12
  705.6 13.3 %collective-permute-start.1 = (bf16[2,128,128]{2,1,0:T(8,128)(2,1)S(1)}, bf16[2,128,128]{2,1,0:T(8,128)(2,1)S(1)}, u32[]{:S(2)}, u32[]{:S(2)}) collective-permute-start(bf16[2,128,128]{2,1,0:T(8,128)(2,1)S(1)} %get-tuple-element.318), channel_id=1, source_target_pairs={{0,8},{8,16},{16,24},{24,32},{32,40},{40,48},{48,56},{56,64},{64,7... | collective-permute-start | bytes 196616 | tf_op jit(solution)/shard_map/while/body/eval_jaxpr/ppermute | solution.py:12
  719.6 13.3 %collective-permute-start.1 = (bf16[2,128,128]{2,1,0:T(8,128)(2,1)S(1)}, bf16[2,128,128]{2,1,0:T(8,128)(2,1)S(1)}, u32[]{:S(2)}, u32[]{:S(2)}) collective-permute-start(bf16[2,128,128]{2,1,0:T(8,128)(2,1)S(1)} %get-tuple-element.318), channel_id=1, source_target_pairs={{0,8},{8,16},{16,24},{24,32},{32,40},{40,48},{48,56},{56,64},{64,7... | collective-permute-start | bytes 196616 | tf_op jit(solution)/shard_map/while/body/eval_jaxpr/ppermute | solution.py:12
  733.5 13.3 %collective-permute-start.1 = (bf16[2,128,128]{2,1,0:T(8,128)(2,1)S(1)}, bf16[2,128,128]{2,1,0:T(8,128)(2,1)S(1)}, u32[]{:S(2)}, u32[]{:S(2)}) collective-permute-start(bf16[2,128,128]{2,1,0:T(8,128)(2,1)S(1)} %get-tuple-element.318), channel_id=1, source_target_pairs={{0,8},{8,16},{16,24},{24,32},{32,40},{40,48},{48,56},{56,64},{64,7... | collective-permute-start | bytes 196616 | tf_op jit(solution)/shard_map/while/body/eval_jaxpr/ppermute | solution.py:12
  747.4 13.3 %collective-permute-start.1 = (bf16[2,128,128]{2,1,0:T(8,128)(2,1)S(1)}, bf16[2,128,128]{2,1,0:T(8,128)(2,1)S(1)}, u32[]{:S(2)}, u32[]{:S(2)}) collective-permute-start(bf16[2,128,128]{2,1,0:T(8,128)(2,1)S(1)} %get-tuple-element.318), channel_id=1, source_target_pairs={{0,8},{8,16},{16,24},{24,32},{32,40},{40,48},{48,56},{56,64},{64,7... | collective-permute-start | bytes 196616 | tf_op jit(solution)/shard_map/while/body/eval_jaxpr/ppermute | solution.py:12
  817.0 13.3 %collective-permute-start.1 = (bf16[2,128,128]{2,1,0:T(8,128)(2,1)S(1)}, bf16[2,128,128]{2,1,0:T(8,128)(2,1)S(1)}, u32[]{:S(2)}, u32[]{:S(2)}) collective-permute-start(bf16[2,128,128]{2,1,0:T(8,128)(2,1)S(1)} %get-tuple-element.318), channel_id=1, source_target_pairs={{0,8},{8,16},{16,24},{24,32},{32,40},{40,48},{48,56},{56,64},{64,7... | collective-permute-start | bytes 196616 | tf_op jit(solution)/shard_map/while/body/eval_jaxpr/ppermute | solution.py:12
  830.9 13.3 %collective-permute-start.1 = (bf16[2,128,128]{2,1,0:T(8,128)(2,1)S(1)}, bf16[2,128,128]{2,1,0:T(8,128)(2,1)S(1)}, u32[]{:S(2)}, u32[]{:S(2)}) collective-permute-start(bf16[2,128,128]{2,1,0:T(8,128)(2,1)S(1)} %get-tuple-element.318), channel_id=1, source_target_pairs={{0,8},{8,16},{16,24},{24,32},{32,40},{40,48},{48,56},{56,64},{64,7... | collective-permute-start | bytes 196616 | tf_op jit(solution)/shard_map/while/body/eval_jaxpr/ppermute | solution.py:12
  844.9 13.3 %collective-permute-start.1 = (bf16[2,128,128]{2,1,0:T(8,128)(2,1)S(1)}, bf16[2,128,128]{2,1,0:T(8,128)(2,1)S(1)}, u32[]{:S(2)}, u32[]{:S(2)}) collective-permute-start(bf16[2,128,128]{2,1,0:T(8,128)(2,1)S(1)} %get-tuple-element.318), channel_id=1, source_target_pairs={{0,8},{8,16},{16,24},{24,32},{32,40},{40,48},{48,56},{56,64},{64,7... | collective-permute-start | bytes 196616 | tf_op jit(solution)/shard_map/while/body/eval_jaxpr/ppermute | solution.py:12
  858.8 13.3 %collective-permute-start.1 = (bf16[2,128,128]{2,1,0:T(8,128)(2,1)S(1)}, bf16[2,128,128]{2,1,0:T(8,128)(2,1)S(1)}, u32[]{:S(2)}, u32[]{:S(2)}) collective-permute-start(bf16[2,128,128]{2,1,0:T(8,128)(2,1)S(1)} %get-tuple-element.318), channel_id=1, source_target_pairs={{0,8},{8,16},{16,24},{24,32},{32,40},{40,48},{48,56},{56,64},{64,7... | collective-permute-start | bytes 196616 | tf_op jit(solution)/shard_map/while/body/eval_jaxpr/ppermute | solution.py:12
  (100 other events, 2743.7 us)
Sparse Core Ops, SparseCore 0:
  10.8 85.6 all-gather.2
  98.5 65.5 all-gather.4
where the time goes:
time: 1090 us; the launch traced here: 1080 us
  waiting for transfers between devices  494 us (45%)
  starting transfers between devices  302 us (28%)
  loops' own time  196 us (18%)
  other arithmetic  50.1 us (5%)
  local copies, waits for them, and re-layouts  16.1 us (1%)
  between operations  14.9 us (1%)
  matrix products  11.9 us (1%)
    ppermute x126, waiting for transfers between devices, passed_along(): lax.ppermute(value, axis, [(source, source + steps) for source in range(l...  340 us
    ppermute x126, starting transfers between devices, passed_along(): lax.ppermute(value, axis, [(source, source + steps) for source in range(l...  302 us
    another operation x1, loops' own time, per_device(): lax.fori_loop(0, lax.axis_size('ctx') - 1, hand_round, (own_pair, start_p...  194 us
    all_gather x1, waiting for transfers between devices, per_device(): lax.all_gather(w_qkv, 'ctx', axis=1, tiled=True)  84.4 us
    all_gather x1, waiting for transfers between devices, per_device(): whole = lax.all_gather(tokens, 'head', axis=1, tiled=True)  67.6 us
    add x63, other arithmetic, combine(): later_state + jnp.where(linked, first_state, 0.0)  40.5 us
  transfers between devices with their start and end apart: 128, of which 65 were waited for; matrix products, arithmetic and copies ran while one was open for 0% of the time, Pallas kernels for 0%

commit v1 on v0

--- a/solution.py
+++ b/solution.py
@@ -4,6 +4,19 @@
 from jax.sharding import PartitionSpec as P
 
 HEAD_DIM = 128
+
+
+def gather_around(value, axis, dim):
+    ways = lax.axis_size(axis)
+    up = [(d, (d + 1) % ways) for d in range(ways)]
+    down = [(d, (d - 1) % ways) for d in range(ways)]
+    earlier, later = ([value], [value])
+    for _ in range(ways // 2):
+        earlier.append(lax.ppermute(earlier[-1], axis, up))
+    for _ in range((ways - 1) // 2):
+        later.append(lax.ppermute(later[-1], axis, down))
+    line = jnp.concatenate([*earlier[::-1], *later[1:]], axis=dim)
+    return jnp.roll(line, (lax.axis_index(axis) - ways // 2) * value.shape[dim], axis=dim)
 
 
 def passed_along(value, axis, steps):
@@ -67,7 +80,7 @@
 
 
 def per_device(tokens, w_qkv, out_gain, seg_ids):
-    whole = lax.all_gather(tokens, "head", axis=1, tiled=True)
+    whole = gather_around(tokens, "head", 1)
     projected = jnp.einsum(
         "tr,grc->gtc",
         whole,

time: 1090 us -> 1020 us (0.936)
  waiting for transfers between devices: 494 us -> 385 us
  starting transfers between devices: 302 us -> 326 us
  local copies, waits for them, and re-layouts: 16.1 us -> 34 us
    all_gather x1, waiting for transfers between devices: 84.4 us -> 2.85 us  [per_device(): lax.all_gather(w_qkv, 'ctx', axis=1, tiled=True)]
    all_gather x1 -> x0, waiting for transfers between devices: 67.6 us -> none  [per_device(): whole = lax.all_gather(tokens, 'head', axis=1, tiled=True)]
    ppermute x0 -> x7, waiting for transfers between devices: none -> 39.9 us  [the longest x4 39.9 us: gather_around(): earlier.append(lax.ppermute(earlier[-1], axis, up))]
    ppermute x0 -> x7, starting transfers between devices: none -> 25.4 us  [the longest x3 15.4 us: gather_around(): later.append(lax.ppermute(later[-1], axis, down))]
    unnamed x9 -> x26, local copies, waits for them, and re-layouts: 0.31 us -> 17.4 us
  transfers between devices with their start and end apart: 128 -> 134, of which waited for: 65 -> 68; matrix products, arithmetic and copies ran while one was open for 0% -> 2% of each run, Pallas kernels for 0% -> 0%
where the time goes in v1:
time: 1020 us; the launch traced here: 1010 us
  waiting for transfers between devices  385 us (38%)
  starting transfers between devices  326 us (32%)
  loops' own time  189 us (19%)
  other arithmetic  49.3 us (5%)
  local copies, waits for them, and re-layouts  34 us (3%)
  between operations  14.8 us (1%)
  matrix products  12.3 us (1%)
    ppermute x126, waiting for transfers between devices, passed_along(): lax.ppermute(value, axis, [(source, source + steps) for source in range(l...  342 us
    ppermute x126, starting transfers between devices, passed_along(): lax.ppermute(value, axis, [(source, source + steps) for source in range(l...  301 us
    another operation x1, loops' own time, per_device(): lax.fori_loop(0, lax.axis_size('ctx') - 1, hand_round, (own_pair, start_p...  188 us
    ppermute x4, waiting for transfers between devices, gather_around(): earlier.append(lax.ppermute(earlier[-1], axis, up))  39.9 us
    add x63, other arithmetic, combine(): later_state + jnp.where(linked, first_state, 0.0)  39.8 us
  transfers between devices with their start and end apart: 134, of which 68 were waited for; matrix products, arithmetic and copies ran while one was open for 2% of the time, Pallas kernels for 0%

profile of v1, /device:TPU:32, one launch (start us, length us, event | category | flops | bytes accessed | tf_op | source)
XLA Modules:
  0.0 1010.8 jit_solution(15903880386415833679)
XLA Ops:
  11.5 18.8 %collective-permute-done.2 = bf16[1024,256]{1,0:T(8,128)(2,1)S(1)} collective-permute-done((bf16[1024,256]{1,0:T(8,128)(2,1)}, bf16[1024,256]{1,0:T(8,128)(2,1)S(1)}, u32[]{:S(2)}, u32[]{:S(2)}) %collective-permute-start.2) | collective-permute-done | bytes 524320 | tf_op jit(solution)/shard_map/ppermute | solution.py:15
  37.4 9.1 collective-permute-done.3
  53.6 8.2 collective-permute-done.4
  96.4 6.6 fusion.16
  109.6 870.3 %while.28 = (s32[]{:T(128)}, bf16[2,128,128]{2,1,0:T(8,128)(2,1)S(1)}, bf16[]{:T(256)}, bf16[2,128,128]{2,1,0:T(8,128)(2,1)}, f32[]{:T(128)}, /*index=5*/f32[]{:...) while((s32[]{:T(128)}, bf16[2,128,128]{2,1,0:T(8,128)(2,1)S(1)}, bf16[]{:T(256)}, ...), condition=%wide.region_3.4_spmd, body=%wide.region_2.3_spmd.sunk | while | flops 163846 | bytes 590031 | solution.py:103
  114.7 5.4 collective-permute-done
  128.5 5.4 collective-permute-done
  142.3 5.4 collective-permute-done
  156.1 5.4 collective-permute-done
  183.8 5.4 collective-permute-done
  197.6 5.4 collective-permute-done
  225.2 5.4 collective-permute-done
  239.0 5.4 collective-permute-done
  266.6 5.4 collective-permute-done
  280.4 5.4 collective-permute-done
  308.0 5.4 collective-permute-done
  321.8 5.4 collective-permute-done
  335.7 5.4 collective-permute-done
  349.5 5.4 collective-permute-done
  363.3 5.4 collective-permute-done
  377.1 5.4 collective-permute-done
  390.9 5.4 collective-permute-done
  404.7 5.4 collective-permute-done
  418.5 5.4 collective-permute-done
  446.1 5.4 collective-permute-done
  459.9 5.4 collective-permute-done
  487.6 5.4 collective-permute-done
  501.4 5.4 collective-permute-done
  529.0 5.4 collective-permute-done
  542.8 5.4 collective-permute-done
  570.4 5.4 collective-permute-done
  982.2 19.3 %while.29 = (s32[]{:T(128)}, f32[2,512,2,128]{1,0,3,2:T(2,128)S(1)}, s32[2]{0:T(128)S(1)}, f32[1024]{0:T(1024)S(1)}, bf16[1024,2,128]{2,1,0:T(2,128)(2,1)S(1)}, ...) while((s32[]{:T(128)}, ...), condition=%wide.region_1.2_spmd.clone, body=%wide.region_0.1_spmd.clone.sunk | while | flops 540541440 | bytes 5519543 | solution.py:75
  (364 shorter events, 623.1 us)
Async XLA Ops:
  6.5 89.9 %all-gather.2.cloned.1.call-start = ((), (), s32[]{:S(2)}) async-start(), calls=%async_computation | async-start | bytes 3194880 | tf_op jit(solution)/shard_map/all_gather | solution.py:87
  7.3 23.1 %collective-permute-start.2 = (bf16[1024,256]{1,0:T(8,128)(2,1)}, bf16[1024,256]{1,0:T(8,128)(2,1)S(1)}, u32[]{:S(2)}, u32[]{:S(2)}) collective-permute-start(bf16[1024,256]{1,0:T(8,128)(2,1)} %param.8), channel_id=1, source_target_pairs={{0,1},{1,2},{2,3},{3,4},{4,5},{5,6},{6,7},{7,0},{8,9},{9,10},{10,1... | collective-permute-start | bytes 1572872 | tf_op jit(solution)/shard_map/ppermute | solution.py:15
  30.3 16.2 %collective-permute-start.3 = (bf16[1024,256]{1,0:T(8,128)(2,1)S(1)}, bf16[1024,256]{1,0:T(8,128)(2,1)S(1)}, u32[]{:S(2)}, u32[]{:S(2)}) collective-permute-start(bf16[1024,256]{1,0:T(8,128)(2,1)S(1)} %collective-permute-done.2), channel_id=1, source_target_pairs={{0,1},{1,2},{2,3},{3,4},{4,5},{5,6},{6,7},{7,0},{8,9},{9,10},{10,1... | collective-permute-start | bytes 1572872 | tf_op jit(solution)/shard_map/ppermute | solution.py:15
  32.3 16.2 %collective-permute-start.6 = (bf16[1024,256]{1,0:T(8,128)(2,1)}, bf16[1024,256]{1,0:T(8,128)(2,1)S(1)}, u32[]{:S(2)}, u32[]{:S(2)}) collective-permute-start(bf16[1024,256]{1,0:T(8,128)(2,1)} %param.8), channel_id=1, source_target_pairs={{0,7},{1,0},{2,1},{3,2},{4,3},{5,4},{6,5},{7,6},{8,15},{9,8},{10,9... | collective-permute-start | bytes 1572872 | tf_op jit(solution)/shard_map/ppermute | solution.py:17
  46.5 15.3 %collective-permute-start.4 = (bf16[1024,256]{1,0:T(8,128)(2,1)S(1)}, bf16[1024,256]{1,0:T(8,128)(2,1)S(1)}, u32[]{:S(2)}, u32[]{:S(2)}) collective-permute-start(bf16[1024,256]{1,0:T(8,128)(2,1)S(1)} %collective-permute-done.3), channel_id=1, source_target_pairs={{0,1},{1,2},{2,3},{3,4},{4,5},{5,6},{6,7},{7,0},{8,9},{9,10},{10,1... | collective-permute-start | bytes 1572872 | tf_op jit(solution)/shard_map/ppermute | solution.py:15
  48.5 18.9 %collective-permute-start.7 = (bf16[1024,256]{1,0:T(8,128)(2,1)S(1)}, bf16[1024,256]{1,0:T(8,128)(2,1)S(1)}, u32[]{:S(2)}, u32[]{:S(2)}) collective-permute-start(bf16[1024,256]{1,0:T(8,128)(2,1)S(1)} %collective-permute-done.6), channel_id=1, source_target_pairs={{0,7},{1,0},{2,1},{3,2},{4,3},{5,4},{6,5},{7,6},{8,15},{9,8},{10,9... | collective-permute-start | bytes 1572872 | tf_op jit(solution)/shard_map/ppermute | solution.py:17
  61.8 14.5 %collective-permute-start.5 = (bf16[1024,256]{1,0:T(8,128)(2,1)S(1)}, bf16[1024,256]{1,0:T(8,128)(2,1)}, u32[]{:S(2)}, u32[]{:S(2)}) collective-permute-start(bf16[1024,256]{1,0:T(8,128)(2,1)S(1)} %collective-permute-done.4), channel_id=1, source_target_pairs={{0,1},{1,2},{2,3},{3,4},{4,5},{5,6},{6,7},{7,0},{8,9},{9,10},{10,1... | collective-permute-start | bytes 1572872 | tf_op jit(solution)/shard_map/ppermute | solution.py:15
  67.4 17.2 %collective-permute-start.8 = (bf16[1024,256]{1,0:T(8,128)(2,1)S(1)}, bf16[1024,256]{1,0:T(8,128)(2,1)S(1)}, u32[]{:S(2)}, u32[]{:S(2)}) collective-permute-start(bf16[1024,256]{1,0:T(8,128)(2,1)S(1)} %collective-permute-done.7), channel_id=1, source_target_pairs={{0,7},{1,0},{2,1},{3,2},{4,3},{5,4},{6,5},{7,6},{8,15},{9,8},{10,9... | collective-permute-start | bytes 1572872 | tf_op jit(solution)/shard_map/ppermute | solution.py:17
  109.7 13.4 %collective-permute-start.1 = (bf16[2,128,128]{2,1,0:T(8,128)(2,1)S(1)}, bf16[2,128,128]{2,1,0:T(8,128)(2,1)S(1)}, u32[]{:S(2)}, u32[]{:S(2)}) collective-permute-start(bf16[2,128,128]{2,1,0:T(8,128)(2,1)S(1)} %get-tuple-element.318), channel_id=1, source_target_pairs={{0,8},{8,16},{16,24},{24,32},{32,40},{40,48},{48,56},{56,64},{64,7... | collective-permute-start | bytes 196616 | tf_op jit(solution)/shard_map/while/body/eval_jaxpr/ppermute | solution.py:25
  137.5 13.2 %collective-permute-start.1 = (bf16[2,128,128]{2,1,0:T(8,128)(2,1)S(1)}, bf16[2,128,128]{2,1,0:T(8,128)(2,1)S(1)}, u32[]{:S(2)}, u32[]{:S(2)}) collective-permute-start(bf16[2,128,128]{2,1,0:T(8,128)(2,1)S(1)} %get-tuple-element.318), channel_id=1, source_target_pairs={{0,8},{8,16},{16,24},{24,32},{32,40},{40,48},{48,56},{56,64},{64,7... | collective-permute-start | bytes 196616 | tf_op jit(solution)/shard_map/while/body/eval_jaxpr/ppermute | solution.py:25
  179.0 13.2 %collective-permute-start.1 = (bf16[2,128,128]{2,1,0:T(8,128)(2,1)S(1)}, bf16[2,128,128]{2,1,0:T(8,128)(2,1)S(1)}, u32[]{:S(2)}, u32[]{:S(2)}) collective-permute-start(bf16[2,128,128]{2,1,0:T(8,128)(2,1)S(1)} %get-tuple-element.318), channel_id=1, source_target_pairs={{0,8},{8,16},{16,24},{24,32},{32,40},{40,48},{48,56},{56,64},{64,7... | collective-permute-start | bytes 196616 | tf_op jit(solution)/shard_map/while/body/eval_jaxpr/ppermute | solution.py:25
  220.4 13.2 %collective-permute-start.1 = (bf16[2,128,128]{2,1,0:T(8,128)(2,1)S(1)}, bf16[2,128,128]{2,1,0:T(8,128)(2,1)S(1)}, u32[]{:S(2)}, u32[]{:S(2)}) collective-permute-start(bf16[2,128,128]{2,1,0:T(8,128)(2,1)S(1)} %get-tuple-element.318), channel_id=1, source_target_pairs={{0,8},{8,16},{16,24},{24,32},{32,40},{40,48},{48,56},{56,64},{64,7... | collective-permute-start | bytes 196616 | tf_op jit(solution)/shard_map/while/body/eval_jaxpr/ppermute | solution.py:25
  261.8 13.2 %collective-permute-start.1 = (bf16[2,128,128]{2,1,0:T(8,128)(2,1)S(1)}, bf16[2,128,128]{2,1,0:T(8,128)(2,1)S(1)}, u32[]{:S(2)}, u32[]{:S(2)}) collective-permute-start(bf16[2,128,128]{2,1,0:T(8,128)(2,1)S(1)} %get-tuple-element.318), channel_id=1, source_target_pairs={{0,8},{8,16},{16,24},{24,32},{32,40},{40,48},{48,56},{56,64},{64,7... | collective-permute-start | bytes 196616 | tf_op jit(solution)/shard_map/while/body/eval_jaxpr/ppermute | solution.py:25
  275.6 13.2 %collective-permute-start.1 = (bf16[2,128,128]{2,1,0:T(8,128)(2,1)S(1)}, bf16[2,128,128]{2,1,0:T(8,128)(2,1)S(1)}, u32[]{:S(2)}, u32[]{:S(2)}) collective-permute-start(bf16[2,128,128]{2,1,0:T(8,128)(2,1)S(1)} %get-tuple-element.318), channel_id=1, source_target_pairs={{0,8},{8,16},{16,24},{24,32},{32,40},{40,48},{48,56},{56,64},{64,7... | collective-permute-start | bytes 196616 | tf_op jit(solution)/shard_map/while/body/eval_jaxpr/ppermute | solution.py:25
  317.1 13.2 %collective-permute-start.1 = (bf16[2,128,128]{2,1,0:T(8,128)(2,1)S(1)}, bf16[2,128,128]{2,1,0:T(8,128)(2,1)S(1)}, u32[]{:S(2)}, u32[]{:S(2)}) collective-permute-start(bf16[2,128,128]{2,1,0:T(8,128)(2,1)S(1)} %get-tuple-element.318), channel_id=1, source_target_pairs={{0,8},{8,16},{16,24},{24,32},{32,40},{40,48},{48,56},{56,64},{64,7... | collective-permute-start | bytes 196616 | tf_op jit(solution)/shard_map/while/body/eval_jaxpr/ppermute | solution.py:25
  358.5 13.2 %collective-permute-start.1 = (bf16[2,128,128]{2,1,0:T(8,128)(2,1)S(1)}, bf16[2,128,128]{2,1,0:T(8,128)(2,1)S(1)}, u32[]{:S(2)}, u32[]{:S(2)}) collective-permute-start(bf16[2,128,128]{2,1,0:T(8,128)(2,1)S(1)} %get-tuple-element.318), channel_id=1, source_target_pairs={{0,8},{8,16},{16,24},{24,32},{32,40},{40,48},{48,56},{56,64},{64,7... | collective-permute-start | bytes 196616 | tf_op jit(solution)/shard_map/while/body/eval_jaxpr/ppermute | solution.py:25
  399.9 13.2 %collective-permute-start.1 = (bf16[2,128,128]{2,1,0:T(8,128)(2,1)S(1)}, bf16[2,128,128]{2,1,0:T(8,128)(2,1)S(1)}, u32[]{:S(2)}, u32[]{:S(2)}) collective-permute-start(bf16[2,128,128]{2,1,0:T(8,128)(2,1)S(1)} %get-tuple-element.318), channel_id=1, source_target_pairs={{0,8},{8,16},{16,24},{24,32},{32,40},{40,48},{48,56},{56,64},{64,7... | collective-permute-start | bytes 196616 | tf_op jit(solution)/shard_map/while/body/eval_jaxpr/ppermute | solution.py:25
  441.4 13.2 %collective-permute-start.1 = (bf16[2,128,128]{2,1,0:T(8,128)(2,1)S(1)}, bf16[2,128,128]{2,1,0:T(8,128)(2,1)S(1)}, u32[]{:S(2)}, u32[]{:S(2)}) collective-permute-start(bf16[2,128,128]{2,1,0:T(8,128)(2,1)S(1)} %get-tuple-element.318), channel_id=1, source_target_pairs={{0,8},{8,16},{16,24},{24,32},{32,40},{40,48},{48,56},{56,64},{64,7... | collective-permute-start | bytes 196616 | tf_op jit(solution)/shard_map/while/body/eval_jaxpr/ppermute | solution.py:25
  482.8 13.2 %collective-permute-start.1 = (bf16[2,128,128]{2,1,0:T(8,128)(2,1)S(1)}, bf16[2,128,128]{2,1,0:T(8,128)(2,1)S(1)}, u32[]{:S(2)}, u32[]{:S(2)}) collective-permute-start(bf16[2,128,128]{2,1,0:T(8,128)(2,1)S(1)} %get-tuple-element.318), channel_id=1, source_target_pairs={{0,8},{8,16},{16,24},{24,32},{32,40},{40,48},{48,56},{56,64},{64,7... | collective-permute-start | bytes 196616 | tf_op jit(solution)/shard_map/while/body/eval_jaxpr/ppermute | solution.py:25
  524.2 13.2 %collective-permute-start.1 = (bf16[2,128,128]{2,1,0:T(8,128)(2,1)S(1)}, bf16[2,128,128]{2,1,0:T(8,128)(2,1)S(1)}, u32[]{:S(2)}, u32[]{:S(2)}) collective-permute-start(bf16[2,128,128]{2,1,0:T(8,128)(2,1)S(1)} %get-tuple-element.318), channel_id=1, source_target_pairs={{0,8},{8,16},{16,24},{24,32},{32,40},{40,48},{48,56},{56,64},{64,7... | collective-permute-start | bytes 196616 | tf_op jit(solution)/shard_map/while/body/eval_jaxpr/ppermute | solution.py:25
  538.0 13.2 %collective-permute-start.1 = (bf16[2,128,128]{2,1,0:T(8,128)(2,1)S(1)}, bf16[2,128,128]{2,1,0:T(8,128)(2,1)S(1)}, u32[]{:S(2)}, u32[]{:S(2)}) collective-permute-start(bf16[2,128,128]{2,1,0:T(8,128)(2,1)S(1)} %get-tuple-element.318), channel_id=1, source_target_pairs={{0,8},{8,16},{16,24},{24,32},{32,40},{40,48},{48,56},{56,64},{64,7... | collective-permute-start | bytes 196616 | tf_op jit(solution)/shard_map/while/body/eval_jaxpr/ppermute | solution.py:25
  579.5 13.2 %collective-permute-start.1 = (bf16[2,128,128]{2,1,0:T(8,128)(2,1)S(1)}, bf16[2,128,128]{2,1,0:T(8,128)(2,1)S(1)}, u32[]{:S(2)}, u32[]{:S(2)}) collective-permute-start(bf16[2,128,128]{2,1,0:T(8,128)(2,1)S(1)} %get-tuple-element.318), channel_id=1, source_target_pairs={{0,8},{8,16},{16,24},{24,32},{32,40},{40,48},{48,56},{56,64},{64,7... | collective-permute-start | bytes 196616 | tf_op jit(solution)/shard_map/while/body/eval_jaxpr/ppermute | solution.py:25
  620.9 13.2 %collective-permute-start.1 = (bf16[2,128,128]{2,1,0:T(8,128)(2,1)S(1)}, bf16[2,128,128]{2,1,0:T(8,128)(2,1)S(1)}, u32[]{:S(2)}, u32[]{:S(2)}) collective-permute-start(bf16[2,128,128]{2,1,0:T(8,128)(2,1)S(1)} %get-tuple-element.318), channel_id=1, source_target_pairs={{0,8},{8,16},{16,24},{24,32},{32,40},{40,48},{48,56},{56,64},{64,7... | collective-permute-start | bytes 196616 | tf_op jit(solution)/shard_map/while/body/eval_jaxpr/ppermute | solution.py:25
  662.3 13.2 %collective-permute-start.1 = (bf16[2,128,128]{2,1,0:T(8,128)(2,1)S(1)}, bf16[2,128,128]{2,1,0:T(8,128)(2,1)S(1)}, u32[]{:S(2)}, u32[]{:S(2)}) collective-permute-start(bf16[2,128,128]{2,1,0:T(8,128)(2,1)S(1)} %get-tuple-element.318), channel_id=1, source_target_pairs={{0,8},{8,16},{16,24},{24,32},{32,40},{40,48},{48,56},{56,64},{64,7... | collective-permute-start | bytes 196616 | tf_op jit(solution)/shard_map/while/body/eval_jaxpr/ppermute | solution.py:25
  703.7 13.2 %collective-permute-start.1 = (bf16[2,128,128]{2,1,0:T(8,128)(2,1)S(1)}, bf16[2,128,128]{2,1,0:T(8,128)(2,1)S(1)}, u32[]{:S(2)}, u32[]{:S(2)}) collective-permute-start(bf16[2,128,128]{2,1,0:T(8,128)(2,1)S(1)} %get-tuple-element.318), channel_id=1, source_target_pairs={{0,8},{8,16},{16,24},{24,32},{32,40},{40,48},{48,56},{56,64},{64,7... | collective-permute-start | bytes 196616 | tf_op jit(solution)/shard_map/while/body/eval_jaxpr/ppermute | solution.py:25
  745.2 13.2 %collective-permute-start.1 = (bf16[2,128,128]{2,1,0:T(8,128)(2,1)S(1)}, bf16[2,128,128]{2,1,0:T(8,128)(2,1)S(1)}, u32[]{:S(2)}, u32[]{:S(2)}) collective-permute-start(bf16[2,128,128]{2,1,0:T(8,128)(2,1)S(1)} %get-tuple-element.318), channel_id=1, source_target_pairs={{0,8},{8,16},{16,24},{24,32},{32,40},{40,48},{48,56},{56,64},{64,7... | collective-permute-start | bytes 196616 | tf_op jit(solution)/shard_map/while/body/eval_jaxpr/ppermute | solution.py:25
  786.6 13.2 %collective-permute-start.1 = (bf16[2,128,128]{2,1,0:T(8,128)(2,1)S(1)}, bf16[2,128,128]{2,1,0:T(8,128)(2,1)S(1)}, u32[]{:S(2)}, u32[]{:S(2)}) collective-permute-start(bf16[2,128,128]{2,1,0:T(8,128)(2,1)S(1)} %get-tuple-element.318), channel_id=1, source_target_pairs={{0,8},{8,16},{16,24},{24,32},{32,40},{40,48},{48,56},{56,64},{64,7... | collective-permute-start | bytes 196616 | tf_op jit(solution)/shard_map/while/body/eval_jaxpr/ppermute | solution.py:25
  800.4 13.2 %collective-permute-start.1 = (bf16[2,128,128]{2,1,0:T(8,128)(2,1)S(1)}, bf16[2,128,128]{2,1,0:T(8,128)(2,1)S(1)}, u32[]{:S(2)}, u32[]{:S(2)}) collective-permute-start(bf16[2,128,128]{2,1,0:T(8,128)(2,1)S(1)} %get-tuple-element.318), channel_id=1, source_target_pairs={{0,8},{8,16},{16,24},{24,32},{32,40},{40,48},{48,56},{56,64},{64,7... | collective-permute-start | bytes 196616 | tf_op jit(solution)/shard_map/while/body/eval_jaxpr/ppermute | solution.py:25
  841.8 13.2 %collective-permute-start.1 = (bf16[2,128,128]{2,1,0:T(8,128)(2,1)S(1)}, bf16[2,128,128]{2,1,0:T(8,128)(2,1)S(1)}, u32[]{:S(2)}, u32[]{:S(2)}) collective-permute-start(bf16[2,128,128]{2,1,0:T(8,128)(2,1)S(1)} %get-tuple-element.318), channel_id=1, source_target_pairs={{0,8},{8,16},{16,24},{24,32},{32,40},{40,48},{48,56},{56,64},{64,7... | collective-permute-start | bytes 196616 | tf_op jit(solution)/shard_map/while/body/eval_jaxpr/ppermute | solution.py:25
  883.3 13.2 %collective-permute-start.1 = (bf16[2,128,128]{2,1,0:T(8,128)(2,1)S(1)}, bf16[2,128,128]{2,1,0:T(8,128)(2,1)S(1)}, u32[]{:S(2)}, u32[]{:S(2)}) collective-permute-start(bf16[2,128,128]{2,1,0:T(8,128)(2,1)S(1)} %get-tuple-element.318), channel_id=1, source_target_pairs={{0,8},{8,16},{16,24},{24,32},{32,40},{40,48},{48,56},{56,64},{64,7... | collective-permute-start | bytes 196616 | tf_op jit(solution)/shard_map/while/body/eval_jaxpr/ppermute | solution.py:25
  924.7 13.2 %collective-permute-start.1 = (bf16[2,128,128]{2,1,0:T(8,128)(2,1)S(1)}, bf16[2,128,128]{2,1,0:T(8,128)(2,1)S(1)}, u32[]{:S(2)}, u32[]{:S(2)}) collective-permute-start(bf16[2,128,128]{2,1,0:T(8,128)(2,1)S(1)} %get-tuple-element.318), channel_id=1, source_target_pairs={{0,8},{8,16},{16,24},{24,32},{32,40},{40,48},{48,56},{56,64},{64,7... | collective-permute-start | bytes 196616 | tf_op jit(solution)/shard_map/while/body/eval_jaxpr/ppermute | solution.py:25
  966.1 13.2 %collective-permute-start.1 = (bf16[2,128,128]{2,1,0:T(8,128)(2,1)S(1)}, bf16[2,128,128]{2,1,0:T(8,128)(2,1)S(1)}, u32[]{:S(2)}, u32[]{:S(2)}) collective-permute-start(bf16[2,128,128]{2,1,0:T(8,128)(2,1)S(1)} %get-tuple-element.318), channel_id=1, source_target_pairs={{0,8},{8,16},{16,24},{24,32},{32,40},{40,48},{48,56},{56,64},{64,7... | collective-permute-start | bytes 196616 | tf_op jit(solution)/shard_map/while/body/eval_jaxpr/ppermute | solution.py:25
  (107 other events, 2915.3 us)
Sparse Core Ops, SparseCore 0:
  10.8 85.6 all-gather.1
